TPU v7x, 128 devices: a whole 4x4x4 slice. The times are simulated.
128 devices in a mesh: chan: 32 (over x, y_lo, z), blk: 4 (over y_hi, core).
Axes of the slice: x: 4, y: 4 (y_hi: 2, y_lo: 2; y = y_hi * 2 + y_lo), z: 4, core: 2. Of those that a mesh axis runs over, the one named last changes fastest.
Arguments:
- voltages: int32 [2048, 134656], P(('chan', 'blk')), may hold values from -128 to 127
- flags: int32 [2048], P(('chan', 'blk')), may hold values 0 or 1
- model_amp: float32 [128, 2048], P('chan'), may hold values from 0.04 to 0.4
- model_phase: float32 [128, 2048], P('chan'), may hold values from -3.140625 to 3.140625
Outputs:
- visibility: bfloat16 [2, 128, 2048, 2048], P(None, 'chan', 'blk')
- gains: float32 [2, 128, 2048], P(None, None, ('chan', 'blk'))
All inputs are finite; a program needn't handle non-finite values. No bound on the sum of `flags` on one device may be relied on, other than what follows from the above.
Results may differ from a plain program's by a relative error of at most 0.0091.
Values may be sent and summed in bfloat16 or wider, within the bound.
No kernel may reach another device: no remote copies, remote signals or barrier semaphores. Data moves between devices by JAX's collectives and lax.ppermute only.
A program may use at most 256 MiB of HBM per device.

v0:
```python
import math
import jax
import jax.numpy as jnp
from jax import lax
from jax.sharding import PartitionSpec as P

CHANS = 128
FRAME = 512
TAPS = 8
BAND_START = 64
SPECTRA = 256
ITERS = 10


def window_table():
    index = jnp.arange(TAPS * FRAME, dtype=jnp.float32)
    offset = (index - TAPS * FRAME / 2 + 0.5) / FRAME
    taper = 0.5 - 0.5 * jnp.cos(2.0 * math.pi * (index + 0.5) / (TAPS * FRAME))
    return (jnp.sinc(offset) * taper).reshape(TAPS, FRAME)


def transform_table():
    sample = jnp.arange(FRAME, dtype=jnp.int32)
    channel = BAND_START + jnp.arange(CHANS, dtype=jnp.int32)
    angle = (sample[:, None] * channel[None, :] % FRAME).astype(jnp.float32) * (
        2.0 * math.pi / FRAME
    )
    return jnp.stack([jnp.cos(angle), -jnp.sin(angle)], axis=1).astype(jnp.bfloat16)


def channelize(voltages, keep):
    window = window_table()
    table = transform_table()
    count = voltages.shape[0]
    samples = voltages.astype(jnp.float32).reshape(count, SPECTRA + TAPS - 1, FRAME)
    frames = window[0] * samples[:, 0:SPECTRA, :]
    for tap in range(1, TAPS):
        frames = frames + window[tap] * samples[:, tap : tap + SPECTRA, :]
    frames = frames.astype(jnp.bfloat16)
    spectra = jnp.einsum("itj,jrc->cirt", frames, table, preferred_element_type=jnp.float32)
    scale = 1.0 / (64.0 * math.sqrt(FRAME))
    return (spectra * (scale * keep)[None, :, None, None]).astype(jnp.bfloat16)


def update_gains(model_re, model_im, power, product_re, product_im):
    denominator = (model_re * model_re + model_im * model_im) * (power[:, None] + 1e-06)
    new_re = (model_re * product_re + model_im * product_im) / denominator
    new_im = (model_re * product_im - model_im * product_re) / denominator
    return (new_re, new_im)


def shards(voltages, flags, model_amp, model_phase):
    keep = (1 - flags).astype(jnp.float32)
    input_count = voltages.shape[0]
    spectra = channelize(voltages, keep)
    blk_count = lax.axis_size("blk")
    block_index = lax.axis_index("blk")
    grouped = lax.all_gather(spectra, "blk", axis=1, tiled=True)
    turned = lax.all_to_all(grouped, "chan", split_axis=0, concat_axis=1, tiled=True)
    local_chans = turned.shape[0]
    all_inputs = turned.shape[1]
    row_count = all_inputs // blk_count
    whole = turned.reshape(local_chans, all_inputs, 2 * SPECTRA)
    rows = lax.dynamic_slice_in_dim(whole, block_index * row_count, row_count, 1)
    rotated = jnp.concatenate([rows[:, :, SPECTRA:], -rows[:, :, :SPECTRA]], axis=2)
    stacked = jnp.stack([rows, rotated])
    correlation = (
        jnp.einsum("rcpk,cqk->rcpq", stacked, whole, preferred_element_type=jnp.float32) / SPECTRA
    )
    visibility = correlation.astype(jnp.bfloat16)
    high = lax.Precision.HIGHEST
    full_re = model_amp * jnp.cos(model_phase)
    full_im = model_amp * jnp.sin(model_phase)
    model_re = lax.dynamic_slice_in_dim(full_re, block_index * row_count, row_count, 1)
    model_im = lax.dynamic_slice_in_dim(full_im, block_index * row_count, row_count, 1)

    def sweep(gain_re, gain_im):
        probe_re = gain_re * model_re - gain_im * model_im
        probe_im = gain_re * model_im + gain_im * model_re
        probes = lax.all_gather(jnp.stack([probe_re, probe_im]), "blk", axis=2, tiled=True)
        power = jnp.sum(probes * probes, axis=(0, 2))
        products = jnp.einsum("rcpq,scq->rscp", correlation, probes, precision=high)
        product_re = products[0, 0] - products[1, 1]
        product_im = products[0, 1] + products[1, 0]
        return update_gains(model_re, model_im, power, product_re, product_im)

    def paired(step_index, carried):
        first_re, first_im = sweep(carried[0], carried[1])
        second_re, second_im = sweep(first_re, first_im)
        return (0.5 * (second_re + first_re), 0.5 * (second_im + first_im))

    start_re = jnp.ones((local_chans, row_count), jnp.float32)
    start_im = jnp.zeros((local_chans, row_count), jnp.float32)
    gain_re, gain_im = lax.fori_loop(0, ITERS // 2, paired, (start_re, start_im))
    solved = lax.all_gather(jnp.stack([gain_re, gain_im]), "blk", axis=2, tiled=True)
    owners = lax.all_to_all(solved, "chan", split_axis=2, concat_axis=1, tiled=True)
    gains = lax.dynamic_slice_in_dim(owners, block_index * input_count, input_count, 2)
    return (visibility, gains)


def solution(mesh):
    return jax.shard_map(
        shards,
        mesh=mesh,
        in_specs=(P(("chan", "blk"), None), P(("chan", "blk")), P("chan", None), P("chan", None)),
        out_specs=(P(None, "chan", "blk", None), P(None, None, ("chan", "blk"))),
        check_vma=False,
    )
```

profile of v0, /device:TPU:1, one launch (start us, length us, event | category | flops | bytes accessed | tf_op | source)
XLA Modules:
  0.0 805.5 jit_solution(235510974840824915)
XLA Ops:
  14.5 10.1 %reshape.358 = f32[16,263,512]{2,1,0:T(8,128)} reshape(f32[16,134656]{1,0:T(8,128)} %convert_element_type.41) | data formatting | bytes 17235968 | tf_op jit(solution)/shard_map/reshape | solution.py:35
  24.6 27.3 %fusion.34 = bf16[128,16,2,256]{3,0,1,2:T(8,128)(2,1)} fusion(f32[16]{0:T(128)S(1)} %convert_multiply_fusion, f32[16,263,512]{2,1,0:T(8,128)} %reshape.358, f32[512]{0:T(512)S(1)} %get-tuple-element.223, f32[512]{0:T(512)S(1)} %get-tuple-element.224, f32[512]{0:T(512)S(1)} %get-tuple-element.225, f32[512]{0:T(512)S(1)} %get-tuple-element.226, ...), kind=kOutput, calls=%fused_computation.70 | convolution fusion | flops 1109917696 | bytes 69484608 | tf_op jit(solution)/shard_map/itj,jrc->cirt/dot_general | solution.py:40
  52.0 66.1 %all-gather.2.cloned.1.call-done = bf16[128,64,2,256]{3,0,1,2:T(8,128)(2,1)} async-done(((bf16[128,16,2,256]{3,0,1,2:T(8,128)(2,1)}), bf16[128,64,2,256]{3,0,1,2:T(8,128)(2,1)}) %all-gather.2.cloned.1.call-update) | async-done | bytes 8388624 | tf_op jit(solution)/shard_map/all_gather | solution.py:58
  118.1 11.5 %copy.43 = bf16[128,64,2,256]{3,1,2,0:T(8,128)(2,1)} copy(bf16[128,64,2,256]{3,0,1,2:T(8,128)(2,1)} %all-gather.2.cloned.1.call-done) | data formatting | bytes 16777216 | tf_op jit(solution)/shard_map/all_gather | solution.py:58
  129.7 7.3 all-to-all-start
  137.8 117.2 %all-to-all-done = bf16[128,64,2,256]{3,1,2,0:T(8,128)(2,1)} async-done(((bf16[128,64,2,256]{3,1,2,0:T(8,128)(2,1)}), bf16[128,64,2,256]{3,1,2,0:T(8,128)(2,1)}, u32[]{:S(2)}, u32[]{:S(2)}) %all-to-all-start) | async-done | bytes 8388640 | tf_op jit(solution)/shard_map/all_to_all | solution.py:59
  254.9 16.4 %copy.81 = bf16[32,4,64,2,256]{4,3,2,0,1:T(2,128)(2,1)} copy(bf16[32,4,64,2,256]{4,2,3,1,0:T(8,128)(2,1)} %bitcast.4) | data formatting | bytes 16777216 | tf_op jit(solution)/shard_map/all_to_all | solution.py:59
  271.4 14.1 %reshape.359 = bf16[4,2048,512]{2,1,0:T(8,128)(2,1)} reshape(bf16[4,32,64,2,256]{4,3,2,1,0:T(2,128)(2,1)} %bitcast.199) | data formatting | bytes 16777216 | tf_op jit(solution)/shard_map/reshape | solution.py:63
  285.4 14.1 %reshape.366 = bf16[4,2048,512,1]{2,1,0,3:T(8,128)(2,1)} reshape(bf16[4,32,64,2,256]{4,3,2,1,0:T(2,128)(2,1)} %bitcast.200) | data formatting | bytes 16777216 | tf_op jit(solution)/shard_map/reshape | solution.py:63
  304.6 22.1 %fusion.78 = (bf16[2,4,512,2048]{2,3,0,1:T(8,128)(2,1)}, f32[2,4,512,2048]{2,3,0,1:T(8,128)}) fusion(bf16[1,4,512,512]{3,2,0,1:T(8,128)(2,1)S(1)} %get-tuple-element.234, bf16[1,4,512,512]{3,2,0,1:T(8,128)(2,1)} %get-tuple-element.235, bf16[4,2048,512,1]{2,1,0,3:T(8,128)(2,1)} %reshape.366), kind=kOutput, calls=%fused_computation.137 | convolution fusion | flops 8615100416 | bytes 62914560 | tf_op jit(solution)/shard_map/rcpk,cqk->rcpq/dot_general | solution.py:68
  326.7 31.8 %copy.45 = f32[2,4,512,2048]{3,2,0,1:T(8,128)} copy(f32[2,4,512,2048]{2,3,0,1:T(8,128)} %get-tuple-element.233) | data formatting | bytes 67108864
  358.5 381.5 %while.16 = (s32[]{:T(128)}, f32[4,512]{1,0:T(4,128)S(1)}, f32[4,512]{1,0:T(4,128)S(1)}, f32[4,512]{1,0:T(4,128)S(1)}, f32[4,512]{1,0:T(4,128)S(1)}, /*index=5*/...) while((s32[]{:T(128)}, f32[4,512]{1,0:T(4,128)S(1)}, ...), condition=%wide.region_3.4_spmd.clone, body=%wide.region_0.3_spmd.clone.sunk | while | flops 402845696 | bytes 68075792 | solution.py:94
  358.6 8.9 %all_gather.24 = f32[2,4,2048]{2,0,1:T(2,128)S(1)} all-gather(f32[2,4,512]{2,0,1:T(2,128)S(1)} %pad_maximum_fusion.5), channel_id=1, replica_groups=mesh['chan'=32,'blk'=4] {'blk'}, dimensions={2}, use_global_device_ids=true | all-gather | bytes 81920 | tf_op jit(solution)/shard_map/while/body/eval_jaxpr/all_gather | solution.py:80
  367.5 30.8 %convolution_bitcast_fusion.2 = f32[2,2,4,512]{3,1,0,2:T(2,128)S(1)} fusion(f32[2,4,512,2048]{3,2,0,1:T(8,128)} %get-tuple-element.328, f32[2,4,2048]{2,0,1:T(2,128)S(1)} %all_gather.24), kind=kOutput, calls=%fused_computation.clone.1 | convolution fusion | flops 201326592 | bytes 33652736 | tf_op jit(solution)/shard_map/while/body/eval_jaxpr/rcpq,scq->rscp/dot_general | solution.py:82
  398.6 6.8 all_gather.25
  405.4 30.8 %fusion.97 = f32[4,2,2,512]{3,1,2,0:T(2,128)S(1)} fusion(f32[2,4,512,2048]{3,2,0,1:T(8,128)} %get-tuple-element.328, f32[2,4,2048,1]{2,1,0,3:T(4,128)S(1)} %bitcast.201), kind=kOutput, calls=%fused_computation.2.clone.1 | convolution fusion | flops 201326592 | bytes 33652736 | tf_op jit(solution)/shard_map/while/body/eval_jaxpr/rcpq,scq->rscp/dot_general | solution.py:82
  436.6 6.8 all_gather.24
  443.3 30.8 %convolution_bitcast_fusion.2 = f32[2,2,4,512]{3,1,0,2:T(2,128)S(1)} fusion(f32[2,4,512,2048]{3,2,0,1:T(8,128)} %get-tuple-element.328, f32[2,4,2048]{2,0,1:T(2,128)S(1)} %all_gather.24), kind=kOutput, calls=%fused_computation.clone.1 | convolution fusion | flops 201326592 | bytes 33652736 | tf_op jit(solution)/shard_map/while/body/eval_jaxpr/rcpq,scq->rscp/dot_general | solution.py:82
  474.5 6.8 all_gather.25
  481.2 30.8 %fusion.97 = f32[4,2,2,512]{3,1,2,0:T(2,128)S(1)} fusion(f32[2,4,512,2048]{3,2,0,1:T(8,128)} %get-tuple-element.328, f32[2,4,2048,1]{2,1,0,3:T(4,128)S(1)} %bitcast.201), kind=kOutput, calls=%fused_computation.2.clone.1 | convolution fusion | flops 201326592 | bytes 33652736 | tf_op jit(solution)/shard_map/while/body/eval_jaxpr/rcpq,scq->rscp/dot_general | solution.py:82
  512.4 6.8 all_gather.24
  519.2 30.8 %convolution_bitcast_fusion.2 = f32[2,2,4,512]{3,1,0,2:T(2,128)S(1)} fusion(f32[2,4,512,2048]{3,2,0,1:T(8,128)} %get-tuple-element.328, f32[2,4,2048]{2,0,1:T(2,128)S(1)} %all_gather.24), kind=kOutput, calls=%fused_computation.clone.1 | convolution fusion | flops 201326592 | bytes 33652736 | tf_op jit(solution)/shard_map/while/body/eval_jaxpr/rcpq,scq->rscp/dot_general | solution.py:82
  550.3 6.8 all_gather.25
  557.0 30.8 %fusion.97 = f32[4,2,2,512]{3,1,2,0:T(2,128)S(1)} fusion(f32[2,4,512,2048]{3,2,0,1:T(8,128)} %get-tuple-element.328, f32[2,4,2048,1]{2,1,0,3:T(4,128)S(1)} %bitcast.201), kind=kOutput, calls=%fused_computation.2.clone.1 | convolution fusion | flops 201326592 | bytes 33652736 | tf_op jit(solution)/shard_map/while/body/eval_jaxpr/rcpq,scq->rscp/dot_general | solution.py:82
  588.2 6.8 all_gather.24
  595.0 30.8 %convolution_bitcast_fusion.2 = f32[2,2,4,512]{3,1,0,2:T(2,128)S(1)} fusion(f32[2,4,512,2048]{3,2,0,1:T(8,128)} %get-tuple-element.328, f32[2,4,2048]{2,0,1:T(2,128)S(1)} %all_gather.24), kind=kOutput, calls=%fused_computation.clone.1 | convolution fusion | flops 201326592 | bytes 33652736 | tf_op jit(solution)/shard_map/while/body/eval_jaxpr/rcpq,scq->rscp/dot_general | solution.py:82
  626.1 6.8 all_gather.25
  632.9 30.8 %fusion.97 = f32[4,2,2,512]{3,1,2,0:T(2,128)S(1)} fusion(f32[2,4,512,2048]{3,2,0,1:T(8,128)} %get-tuple-element.328, f32[2,4,2048,1]{2,1,0,3:T(4,128)S(1)} %bitcast.201), kind=kOutput, calls=%fused_computation.2.clone.1 | convolution fusion | flops 201326592 | bytes 33652736 | tf_op jit(solution)/shard_map/while/body/eval_jaxpr/rcpq,scq->rscp/dot_general | solution.py:82
  670.8 30.8 %convolution_bitcast_fusion.2 = f32[2,2,4,512]{3,1,0,2:T(2,128)S(1)} fusion(f32[2,4,512,2048]{3,2,0,1:T(8,128)} %get-tuple-element.328, f32[2,4,2048]{2,0,1:T(2,128)S(1)} %all_gather.24), kind=kOutput, calls=%fused_computation.clone.1 | convolution fusion | flops 201326592 | bytes 33652736 | tf_op jit(solution)/shard_map/while/body/eval_jaxpr/rcpq,scq->rscp/dot_general | solution.py:82
  708.7 30.8 %fusion.97 = f32[4,2,2,512]{3,1,2,0:T(2,128)S(1)} fusion(f32[2,4,512,2048]{3,2,0,1:T(8,128)} %get-tuple-element.328, f32[2,4,2048,1]{2,1,0,3:T(4,128)S(1)} %bitcast.201), kind=kOutput, calls=%fused_computation.2.clone.1 | convolution fusion | flops 201326592 | bytes 33652736 | tf_op jit(solution)/shard_map/while/body/eval_jaxpr/rcpq,scq->rscp/dot_general | solution.py:82
  751.7 18.3 %all-to-all-start.1 = ((f32[32,1,512]{2,1,0:T(1,128)}), f32[32,1,512]{2,1,0:T(1,128)S(1)}, u32[]{:S(2)}, u32[]{:S(2)}) async-start(f32[32,1,512]{2,1,0:T(1,128)} %reshape.368), calls=%async_computation.1 | async-start | bytes 131072 | tf_op jit(solution)/shard_map/all_to_all | solution.py:96
  770.0 21.5 %copy.48 = bf16[2,4,512,2048]{3,2,1,0:T(8,128)(2,1)} copy(bf16[2,4,512,2048]{2,3,0,1:T(8,128)(2,1)} %get-tuple-element.232) | data formatting | bytes 33554432
  (98 shorter events, 48.8 us)
Async XLA Ops:
  7.2 111.0 %all-gather.2.cloned.1.call-start = ((), (), s32[]{:S(2)}) async-start(), calls=%async_computation.2 | async-start | bytes 10485760 | tf_op jit(solution)/shard_map/all_gather | solution.py:58
  14.5 10.2 %copy-start = (s32[16]{0:T(128)S(1)}, s32[16]{0:T(128)}, u32[]{:S(2)}) copy-start(s32[16]{0:T(128)} %param.7) | copy-start | bytes 196
  129.7 125.3 %all-to-all-start = ((bf16[128,64,2,256]{3,1,2,0:T(8,128)(2,1)}), bf16[128,64,2,256]{3,1,2,0:T(8,128)(2,1)}, u32[]{:S(2)}, u32[]{:S(2)}) async-start(bf16[128,64,2,256]{3,1,2,0:T(8,128)(2,1)} %copy.43), calls=%async_computation | async-start | bytes 16777216 | tf_op jit(solution)/shard_map/all_to_all | solution.py:59
  751.7 39.8 %all-to-all-start.1 = ((f32[32,1,512]{2,1,0:T(1,128)}), f32[32,1,512]{2,1,0:T(1,128)S(1)}, u32[]{:S(2)}, u32[]{:S(2)}) async-start(f32[32,1,512]{2,1,0:T(1,128)} %reshape.368), calls=%async_computation.1 | async-start | bytes 131072 | tf_op jit(solution)/shard_map/all_to_all | solution.py:96
Sparse Core Ops, SparseCore 0:
  52.1 65.9 all-gather.1
where the time goes:
time: 808 us; the launch traced here: 806 us
  matrix products  357 us (44%)
  waiting for transfers between devices  183 us (23%)
  local copies, waits for them, and re-layouts  131 us (16%)
  blocking collectives  76.4 us (9%)
  starting transfers between devices  25.6 us (3%)
  other arithmetic  17 us (2%)
  between operations  14.2 us (2%)
    dot_general x10, matrix products, sweep(): products = jnp.einsum('rcpq,scq->rscp', correlation, probes, precision=high)  308 us
    all_to_all x1, waiting for transfers between devices, shards(): lax.all_to_all(grouped, 'chan', split_axis=0, concat_axis=1, tiled=True)  117 us
    all_gather x10, blocking collectives, sweep(): lax.all_gather(jnp.stack([probe_re, probe_im]), 'blk', axis=2, tiled=True)  69.7 us
    all_gather x1, waiting for transfers between devices, shards(): grouped = lax.all_gather(spectra, 'blk', axis=1, tiled=True)  66.1 us
    unnamed x7, local copies, waits for them, and re-layouts  61 us
    reshape x2, local copies, waits for them, and re-layouts, shards(): whole = turned.reshape(local_chans, all_inputs, 2 * SPECTRA)  28.1 us
    dot_general x1, matrix products, channelize(): jnp.einsum('itj,jrc->cirt', frames, table, preferred_element_type=jnp.flo...  27.3 us
    dot_general x1, matrix products, shards(): jnp.einsum('rcpk,cqk->rcpq', stacked, whole, preferred_element_type=jnp.f...  22.1 us
  transfers between devices with their start and end apart: 3, of which 2 were waited for; matrix products, arithmetic and copies ran while one was open for 3% of the time, Pallas kernels for 0%

commit v1 on v0

--- a/solution.py
+++ b/solution.py
@@ -1,3 +1,4 @@
+import functools
 import math
 import jax
 import jax.numpy as jnp
@@ -10,6 +11,16 @@
 BAND_START = 64
 SPECTRA = 256
 ITERS = 10
+
+
+def _tell_runs(w_in, along_axis):
+    found_now = jnp.concatenate(
+        lax.all_to_all(jnp.stack(lax.axis_size(along_axis) * [w_in]), along_axis, 0, 0), axis=2
+    )
+    return found_now
+
+
+_save_column = functools.partial(_tell_runs, along_axis="blk")
 
 
 def window_table():
@@ -77,7 +88,7 @@
     def sweep(gain_re, gain_im):
         probe_re = gain_re * model_re - gain_im * model_im
         probe_im = gain_re * model_im + gain_im * model_re
-        probes = lax.all_gather(jnp.stack([probe_re, probe_im]), "blk", axis=2, tiled=True)
+        probes = _save_column(jnp.stack([probe_re, probe_im]))
         power = jnp.sum(probes * probes, axis=(0, 2))
         products = jnp.einsum("rcpq,scq->rscp", correlation, probes, precision=high)
         product_re = products[0, 0] - products[1, 1]

time: 808 us -> 830 us (1.027)
  blocking collectives: 76.4 us -> 49.6 us
  waiting for transfers between devices: 183 us -> 207 us
  starting transfers between devices: 25.6 us -> 45.6 us
    all_gather x10 -> x0, blocking collectives: 69.7 us -> none  [sweep(): lax.all_gather(jnp.stack([probe_re, probe_im]), 'blk', axis=2, tiled=True)]
    all_to_all x0 -> x5, blocking collectives: none -> 42.2 us  [_tell_runs(): lax.all_to_all(jnp.stack(lax.axis_size(along_axis) * [w_in]), along_axis,...]
    all_to_all x0 -> x5, waiting for transfers between devices: none -> 23.8 us  [_tell_runs(): lax.all_to_all(jnp.stack(lax.axis_size(along_axis) * [w_in]), along_axis,...]
    all_to_all x0 -> x5, starting transfers between devices: none -> 20.6 us  [_tell_runs(): lax.all_to_all(jnp.stack(lax.axis_size(along_axis) * [w_in]), along_axis,...]
  transfers between devices with their start and end apart: 3 -> 8, of which waited for: 2 -> 7; matrix products, arithmetic and copies ran while one was open for 3% -> 3% of each run, Pallas kernels for 0% -> 0%
where the time goes in v1:
time: 830 us; the launch traced here: 827 us
  matrix products  357 us (43%)
  waiting for transfers between devices  207 us (25%)
  local copies, waits for them, and re-layouts  136 us (16%)
  blocking collectives  49.6 us (6%)
  starting transfers between devices  45.6 us (5%)
  other arithmetic  16.9 us (2%)
  between operations  14.2 us (2%)
    dot_general x10, matrix products, sweep(): products = jnp.einsum('rcpq,scq->rscp', correlation, probes, precision=high)  308 us
    all_to_all x1, waiting for transfers between devices, shards(): lax.all_to_all(grouped, 'chan', split_axis=0, concat_axis=1, tiled=True)  117 us
    all_gather x1, waiting for transfers between devices, shards(): grouped = lax.all_gather(spectra, 'blk', axis=1, tiled=True)  66.1 us
    unnamed x7, local copies, waits for them, and re-layouts  61.2 us
    all_to_all x5, blocking collectives, _tell_runs(): lax.all_to_all(jnp.stack(lax.axis_size(along_axis) * [w_in]), along_axis,...  42.2 us
    reshape x2, local copies, waits for them, and re-layouts, shards(): whole = turned.reshape(local_chans, all_inputs, 2 * SPECTRA)  28.1 us
    dot_general x1, matrix products, channelize(): jnp.einsum('itj,jrc->cirt', frames, table, preferred_element_type=jnp.flo...  27.4 us
    all_to_all x5, waiting for transfers between devices, _tell_runs(): lax.all_to_all(jnp.stack(lax.axis_size(along_axis) * [w_in]), along_axis,...  23.8 us
  transfers between devices with their start and end apart: 8, of which 7 were waited for; matrix products, arithmetic and copies ran while one was open for 3% of the time, Pallas kernels for 0%

profile of v1, /device:TPU:1, one launch (start us, length us, event | category | flops | bytes accessed | tf_op | source)
XLA Modules:
  0.0 826.9 jit_solution(1450118675787675744)
XLA Ops:
  8.6 5.9 convert_element_type.41
  14.5 10.1 %reshape.386 = f32[16,263,512]{2,1,0:T(8,128)} reshape(f32[16,134656]{1,0:T(8,128)} %convert_element_type.41) | data formatting | bytes 17235968 | tf_op jit(solution)/shard_map/reshape | solution.py:46
  24.7 27.4 %fusion.34 = bf16[128,16,2,256]{3,0,1,2:T(8,128)(2,1)} fusion(f32[16]{0:T(128)S(1)} %convert_multiply_fusion, f32[16,263,512]{2,1,0:T(8,128)} %reshape.386, f32[512]{0:T(512)S(1)} %get-tuple-element.223, f32[512]{0:T(512)S(1)} %get-tuple-element.224, f32[512]{0:T(512)S(1)} %get-tuple-element.225, f32[512]{0:T(512)S(1)} %get-tuple-element.226, ...), kind=kOutput, calls=%fused_computation.70 | convolution fusion | flops 1109917696 | bytes 69484608 | tf_op jit(solution)/shard_map/itj,jrc->cirt/dot_general | solution.py:51
  52.0 66.1 %all-gather.2.cloned.1.call-done = bf16[128,64,2,256]{3,0,1,2:T(8,128)(2,1)} async-done(((bf16[128,16,2,256]{3,0,1,2:T(8,128)(2,1)}), bf16[128,64,2,256]{3,0,1,2:T(8,128)(2,1)}) %all-gather.2.cloned.1.call-update) | async-done | bytes 8388624 | tf_op jit(solution)/shard_map/all_gather | solution.py:69
  118.2 11.5 %copy.47 = bf16[128,64,2,256]{3,1,2,0:T(8,128)(2,1)} copy(bf16[128,64,2,256]{3,0,1,2:T(8,128)(2,1)} %all-gather.2.cloned.1.call-done) | data formatting | bytes 16777216 | tf_op jit(solution)/shard_map/all_gather | solution.py:69
  129.7 7.3 all-to-all-start.2
  137.8 117.2 %all-to-all-done.2 = bf16[128,64,2,256]{3,1,2,0:T(8,128)(2,1)} async-done(((bf16[128,64,2,256]{3,1,2,0:T(8,128)(2,1)}), bf16[128,64,2,256]{3,1,2,0:T(8,128)(2,1)}, u32[]{:S(2)}, u32[]{:S(2)}) %all-to-all-start.2) | async-done | bytes 8388640 | tf_op jit(solution)/shard_map/all_to_all | solution.py:70
  255.0 16.4 %copy.81 = bf16[32,4,64,2,256]{4,3,2,0,1:T(2,128)(2,1)} copy(bf16[32,4,64,2,256]{4,2,3,1,0:T(8,128)(2,1)} %bitcast.4) | data formatting | bytes 16777216 | tf_op jit(solution)/shard_map/all_to_all | solution.py:70
  271.4 14.1 %reshape.387 = bf16[4,2048,512]{2,1,0:T(8,128)(2,1)} reshape(bf16[4,32,64,2,256]{4,3,2,1,0:T(2,128)(2,1)} %bitcast.217) | data formatting | bytes 16777216 | tf_op jit(solution)/shard_map/reshape | solution.py:74
  285.5 14.0 %reshape.398 = bf16[4,2048,512,1]{2,1,0,3:T(8,128)(2,1)} reshape(bf16[4,32,64,2,256]{4,3,2,1,0:T(2,128)(2,1)} %bitcast.218) | data formatting | bytes 16777216 | tf_op jit(solution)/shard_map/reshape | solution.py:74
  304.7 22.1 %fusion.78 = (bf16[2,4,512,2048]{2,3,0,1:T(8,128)(2,1)}, f32[2,4,512,2048]{2,3,0,1:T(8,128)}) fusion(bf16[1,4,512,512]{3,2,0,1:T(8,128)(2,1)S(1)} %get-tuple-element.234, bf16[1,4,512,512]{3,2,0,1:T(8,128)(2,1)} %get-tuple-element.235, bf16[4,2048,512,1]{2,1,0,3:T(8,128)(2,1)} %reshape.398), kind=kOutput, calls=%fused_computation.137 | convolution fusion | flops 8615100416 | bytes 62914560 | tf_op jit(solution)/shard_map/rcpk,cqk->rcpq/dot_general | solution.py:79
  326.7 32.0 %copy.49 = f32[2,4,512,2048]{3,2,0,1:T(8,128)} copy(f32[2,4,512,2048]{2,3,0,1:T(8,128)} %get-tuple-element.233) | data formatting | bytes 67108864
  358.7 402.6 %while.16 = (s32[]{:T(128)}, f32[4,512]{1,0:T(4,128)S(1)}, f32[4,512]{1,0:T(4,128)S(1)}, f32[4,512]{1,0:T(4,128)S(1)}, f32[4,512]{1,0:T(4,128)S(1)}, /*index=5*/...) while((s32[]{:T(128)}, f32[4,512]{1,0:T(4,128)S(1)}, ...), condition=%wide.region_3.4_spmd.clone, body=%wide.region_0.3_spmd.clone.sunk | while | flops 402845696 | bytes 68960560 | solution.py:105
  358.8 10.2 %all_to_all.53 = f32[4,2,4,512]{3,1,2,0:T(2,128)S(1)} all-to-all(f32[4,2,4,512]{3,1,2,0:T(2,128)S(1)} %stack.79), channel_id=1, replica_groups=mesh['chan'=32,'blk'=4] {'blk'}, dimensions={0} | all-to-all | bytes 131072 | tf_op jit(solution)/shard_map/while/body/eval_jaxpr/all_to_all | solution.py:18
  369.1 30.8 %convolution_bitcast_fusion.2 = f32[2,2,4,512]{3,1,0,2:T(2,128)S(1)} fusion(f32[2,4,512,2048]{3,2,0,1:T(8,128)} %get-tuple-element.328, f32[2,4,2048,1]{2,0,1,3:T(2,128)S(1)} %reshape.406), kind=kOutput, calls=%fused_computation.clone.1 | convolution fusion | flops 201326592 | bytes 33652736 | tf_op jit(solution)/shard_map/while/body/eval_jaxpr/rcpq,scq->rscp/dot_general | solution.py:93
  409.9 30.8 %fusion.97 = f32[4,2,2,512]{3,1,2,0:T(2,128)S(1)} fusion(f32[2,4,512,2048]{3,2,0,1:T(8,128)} %get-tuple-element.328, f32[2,4,2048,1]{2,0,1,3:T(2,128)S(1)} %reshape.407), kind=kOutput, calls=%fused_computation.1.clone.1 | convolution fusion | flops 201326592 | bytes 33652736 | tf_op jit(solution)/shard_map/while/body/eval_jaxpr/rcpq,scq->rscp/dot_general | solution.py:93
  441.0 8.0 all_to_all.53
  449.1 30.8 %convolution_bitcast_fusion.2 = f32[2,2,4,512]{3,1,0,2:T(2,128)S(1)} fusion(f32[2,4,512,2048]{3,2,0,1:T(8,128)} %get-tuple-element.328, f32[2,4,2048,1]{2,0,1,3:T(2,128)S(1)} %reshape.406), kind=kOutput, calls=%fused_computation.clone.1 | convolution fusion | flops 201326592 | bytes 33652736 | tf_op jit(solution)/shard_map/while/body/eval_jaxpr/rcpq,scq->rscp/dot_general | solution.py:93
  489.9 30.8 %fusion.97 = f32[4,2,2,512]{3,1,2,0:T(2,128)S(1)} fusion(f32[2,4,512,2048]{3,2,0,1:T(8,128)} %get-tuple-element.328, f32[2,4,2048,1]{2,0,1,3:T(2,128)S(1)} %reshape.407), kind=kOutput, calls=%fused_computation.1.clone.1 | convolution fusion | flops 201326592 | bytes 33652736 | tf_op jit(solution)/shard_map/while/body/eval_jaxpr/rcpq,scq->rscp/dot_general | solution.py:93
  521.1 8.0 all_to_all.53
  529.2 30.8 %convolution_bitcast_fusion.2 = f32[2,2,4,512]{3,1,0,2:T(2,128)S(1)} fusion(f32[2,4,512,2048]{3,2,0,1:T(8,128)} %get-tuple-element.328, f32[2,4,2048,1]{2,0,1,3:T(2,128)S(1)} %reshape.406), kind=kOutput, calls=%fused_computation.clone.1 | convolution fusion | flops 201326592 | bytes 33652736 | tf_op jit(solution)/shard_map/while/body/eval_jaxpr/rcpq,scq->rscp/dot_general | solution.py:93
  565.1 4.8 all-to-all-done.1
  570.0 30.8 %fusion.97 = f32[4,2,2,512]{3,1,2,0:T(2,128)S(1)} fusion(f32[2,4,512,2048]{3,2,0,1:T(8,128)} %get-tuple-element.328, f32[2,4,2048,1]{2,0,1,3:T(2,128)S(1)} %reshape.407), kind=kOutput, calls=%fused_computation.1.clone.1 | convolution fusion | flops 201326592 | bytes 33652736 | tf_op jit(solution)/shard_map/while/body/eval_jaxpr/rcpq,scq->rscp/dot_general | solution.py:93
  601.1 8.0 all_to_all.53
  609.2 30.8 %convolution_bitcast_fusion.2 = f32[2,2,4,512]{3,1,0,2:T(2,128)S(1)} fusion(f32[2,4,512,2048]{3,2,0,1:T(8,128)} %get-tuple-element.328, f32[2,4,2048,1]{2,0,1,3:T(2,128)S(1)} %reshape.406), kind=kOutput, calls=%fused_computation.clone.1 | convolution fusion | flops 201326592 | bytes 33652736 | tf_op jit(solution)/shard_map/while/body/eval_jaxpr/rcpq,scq->rscp/dot_general | solution.py:93
  650.0 30.8 %fusion.97 = f32[4,2,2,512]{3,1,2,0:T(2,128)S(1)} fusion(f32[2,4,512,2048]{3,2,0,1:T(8,128)} %get-tuple-element.328, f32[2,4,2048,1]{2,0,1,3:T(2,128)S(1)} %reshape.407), kind=kOutput, calls=%fused_computation.1.clone.1 | convolution fusion | flops 201326592 | bytes 33652736 | tf_op jit(solution)/shard_map/while/body/eval_jaxpr/rcpq,scq->rscp/dot_general | solution.py:93
  681.2 8.0 all_to_all.53
  689.3 30.8 %convolution_bitcast_fusion.2 = f32[2,2,4,512]{3,1,0,2:T(2,128)S(1)} fusion(f32[2,4,512,2048]{3,2,0,1:T(8,128)} %get-tuple-element.328, f32[2,4,2048,1]{2,0,1,3:T(2,128)S(1)} %reshape.406), kind=kOutput, calls=%fused_computation.clone.1 | convolution fusion | flops 201326592 | bytes 33652736 | tf_op jit(solution)/shard_map/while/body/eval_jaxpr/rcpq,scq->rscp/dot_general | solution.py:93
  730.1 30.8 %fusion.97 = f32[4,2,2,512]{3,1,2,0:T(2,128)S(1)} fusion(f32[2,4,512,2048]{3,2,0,1:T(8,128)} %get-tuple-element.328, f32[2,4,2048,1]{2,0,1,3:T(2,128)S(1)} %reshape.407), kind=kOutput, calls=%fused_computation.1.clone.1 | convolution fusion | flops 201326592 | bytes 33652736 | tf_op jit(solution)/shard_map/while/body/eval_jaxpr/rcpq,scq->rscp/dot_general | solution.py:93
  761.3 7.4 all_gather.7
  773.7 17.7 %all-to-all-start.3 = ((f32[32,1,512]{2,1,0:T(1,128)}), f32[32,1,512]{2,1,0:T(1,128)S(1)}, u32[]{:S(2)}, u32[]{:S(2)}) async-start(f32[32,1,512]{2,1,0:T(1,128)} %reshape.402), calls=%async_computation.3 | async-start | bytes 131072 | tf_op jit(solution)/shard_map/all_to_all | solution.py:107
  791.4 21.5 %copy.52 = bf16[2,4,512,2048]{3,2,1,0:T(8,128)(2,1)} copy(bf16[2,4,512,2048]{2,3,0,1:T(8,128)(2,1)} %get-tuple-element.232) | data formatting | bytes 33554432
  (133 shorter events, 66.6 us)
Async XLA Ops:
  7.2 111.0 %all-gather.2.cloned.1.call-start = ((), (), s32[]{:S(2)}) async-start(), calls=%async_computation.4 | async-start | bytes 10485760 | tf_op jit(solution)/shard_map/all_gather | solution.py:69
  14.5 10.2 %copy-start = (s32[16]{0:T(128)S(1)}, s32[16]{0:T(128)}, u32[]{:S(2)}) copy-start(s32[16]{0:T(128)} %param.7) | copy-start | bytes 196
  129.7 125.3 %all-to-all-start.2 = ((bf16[128,64,2,256]{3,1,2,0:T(8,128)(2,1)}), bf16[128,64,2,256]{3,1,2,0:T(8,128)(2,1)}, u32[]{:S(2)}, u32[]{:S(2)}) async-start(bf16[128,64,2,256]{3,1,2,0:T(8,128)(2,1)} %copy.47), calls=%async_computation.2 | async-start | bytes 16777216 | tf_op jit(solution)/shard_map/all_to_all | solution.py:70
  400.9 8.9 %all-to-all-start.1 = ((f32[4,2,4,512]{3,1,2,0:T(2,128)}), f32[4,2,4,512]{3,1,2,0:T(2,128)S(1)}, u32[]{:S(2)}, u32[]{:S(2)}) async-start(f32[4,2,4,512]{3,1,2,0:T(2,128)} %stack.80), calls=%async_computation.1 | async-start | bytes 131072 | tf_op jit(solution)/shard_map/while/body/eval_jaxpr/all_to_all | solution.py:18
  480.9 8.9 %all-to-all-start.1 = ((f32[4,2,4,512]{3,1,2,0:T(2,128)}), f32[4,2,4,512]{3,1,2,0:T(2,128)S(1)}, u32[]{:S(2)}, u32[]{:S(2)}) async-start(f32[4,2,4,512]{3,1,2,0:T(2,128)} %stack.80), calls=%async_computation.1 | async-start | bytes 131072 | tf_op jit(solution)/shard_map/while/body/eval_jaxpr/all_to_all | solution.py:18
  561.0 8.9 %all-to-all-start.1 = ((f32[4,2,4,512]{3,1,2,0:T(2,128)}), f32[4,2,4,512]{3,1,2,0:T(2,128)S(1)}, u32[]{:S(2)}, u32[]{:S(2)}) async-start(f32[4,2,4,512]{3,1,2,0:T(2,128)} %stack.80), calls=%async_computation.1 | async-start | bytes 131072 | tf_op jit(solution)/shard_map/while/body/eval_jaxpr/all_to_all | solution.py:18
  641.0 8.9 %all-to-all-start.1 = ((f32[4,2,4,512]{3,1,2,0:T(2,128)}), f32[4,2,4,512]{3,1,2,0:T(2,128)S(1)}, u32[]{:S(2)}, u32[]{:S(2)}) async-start(f32[4,2,4,512]{3,1,2,0:T(2,128)} %stack.80), calls=%async_computation.1 | async-start | bytes 131072 | tf_op jit(solution)/shard_map/while/body/eval_jaxpr/all_to_all | solution.py:18
  721.1 8.9 %all-to-all-start.1 = ((f32[4,2,4,512]{3,1,2,0:T(2,128)}), f32[4,2,4,512]{3,1,2,0:T(2,128)S(1)}, u32[]{:S(2)}, u32[]{:S(2)}) async-start(f32[4,2,4,512]{3,1,2,0:T(2,128)} %stack.80), calls=%async_computation.1 | async-start | bytes 131072 | tf_op jit(solution)/shard_map/while/body/eval_jaxpr/all_to_all | solution.py:18
  773.7 39.2 %all-to-all-start.3 = ((f32[32,1,512]{2,1,0:T(1,128)}), f32[32,1,512]{2,1,0:T(1,128)S(1)}, u32[]{:S(2)}, u32[]{:S(2)}) async-start(f32[32,1,512]{2,1,0:T(1,128)} %reshape.402), calls=%async_computation.3 | async-start | bytes 131072 | tf_op jit(solution)/shard_map/all_to_all | solution.py:107
Sparse Core Ops, SparseCore 0:
  52.2 65.9 all-gather.1
